TPU v7x, 256 devices: a whole 4x4x8 slice. The times are simulated.
256 devices in a mesh: row: 8 (over y_hi, x), col: 32 (over y_lo, z, core).
Axes of the slice: x: 4, y: 4 (y_hi: 2, y_lo: 2; y = y_hi * 2 + y_lo), z: 8, core: 2. Of those that a mesh axis runs over, the one named last changes fastest.
Arguments:
- left_image: bfloat16 [64, 16384, 128], P('row', 'col'), may hold values from -9 to 9
- right_image: bfloat16 [64, 16384, 128], P('row', 'col'), may hold values from -9 to 9
- conv_weight: bfloat16 [3, 3, 128, 256], replicated, may hold values from -0.1875 to 0.1875
Outputs:
- disparity: float32 [32, 8192], P('row', 'col')
- entropy: float32 [32, 8192], P('row', 'col')
All inputs are finite; a program needn't handle non-finite values.
Results may differ from a plain program's by a relative error of at most 0.0057.
Values may be sent and summed in bfloat16 or wider, within the bound.
No kernel may reach another device: no remote copies, remote signals or barrier semaphores. Data moves between devices by JAX's collectives and lax.ppermute only.
A program may use at most 64 MiB of HBM per device.

v0:
```python
import jax
import jax.numpy as jnp
from jax import lax
from jax.sharding import PartitionSpec as P

NEG_FILL = -1e30


def from_behind(array, axis, by):
    count = lax.axis_size(axis)
    pairs = [(i, i + by) for i in range(count) if 0 <= i + by < count]
    return lax.ppermute(array, axis, pairs)


def conv_taps(padded, weights, row_count, col_count):
    total = jnp.zeros((row_count * col_count, weights.shape[-1]), jnp.float32)
    for a in range(3):
        for b in range(3):
            window = padded[a : a + 2 * row_count - 1 : 2, b : b + 2 * col_count - 1 : 2, :]
            total = total + jnp.dot(
                window.reshape(row_count * col_count, -1),
                weights[a, b],
                preferred_element_type=jnp.float32,
            )
    return total.astype(jnp.bfloat16).reshape(row_count, col_count, -1)


def empty_state(row_count, col_count):
    zeros = jnp.zeros((row_count, col_count), jnp.float32)
    return (jnp.full((row_count, col_count), NEG_FILL, jnp.float32), zeros, zeros, zeros)


def absorb(state, query, panel_keys, offset):
    peak, mass, moment, spread = state
    scores = jnp.einsum(
        "rif,rjf->rij", query, panel_keys, preferred_element_type=jnp.float32
    ) * query.shape[-1] ** (-0.5)
    offset = jnp.asarray(offset, jnp.int32).astype(jnp.float32)
    distance = (
        offset
        + jnp.arange(query.shape[1], dtype=jnp.float32)[:, None]
        - jnp.arange(panel_keys.shape[1], dtype=jnp.float32)[None, :]
    )
    allowed = distance >= 0.0
    block_peak = jnp.max(jnp.where(allowed, scores, NEG_FILL), axis=-1)
    new_peak = jnp.maximum(peak, block_peak)
    shifted = jnp.where(allowed, scores - new_peak[:, :, None], NEG_FILL)
    weights = jnp.exp(shifted)
    settled = jnp.where(allowed, shifted, 0.0)
    factor = jnp.exp(peak - new_peak)
    mass_new = mass * factor + jnp.sum(weights, axis=-1)
    moment_new = moment * factor + jnp.sum(weights * distance, axis=-1)
    spread_new = factor * (spread + (peak - new_peak) * mass) + jnp.sum(weights * settled, axis=-1)
    return (new_peak, mass_new, moment_new, spread_new)


def finish(state, col_count):
    disparity = state[2] / state[1] / col_count
    entropy = jnp.log(state[1]) - state[3] / state[1]
    return (disparity, entropy)


def local(left_image, right_image, conv_weight):
    row_count = left_image.shape[0] // 2
    col_count = left_image.shape[1] // 2
    border = jnp.stack([left_image[:, -1:, :], right_image[:, -1:, :]])
    border = from_behind(border, "col", 1)
    left_wide = jnp.concatenate([border[0], left_image], axis=1)
    right_wide = jnp.concatenate([border[1], right_image], axis=1)
    upper = from_behind(jnp.stack([left_wide[-1:], right_wide[-1:]]), "row", 1)
    left_full = jnp.concatenate([upper[0], left_wide], axis=0)
    right_full = jnp.concatenate([upper[1], right_wide], axis=0)
    left_feat = conv_taps(left_full, conv_weight, row_count, col_count)
    right_feat = conv_taps(right_full, conv_weight, row_count, col_count)
    position = lax.axis_index("col")
    start_state = empty_state(row_count, col_count)
    piece = lax.all_gather(right_feat, "col", axis=1, tiled=True)
    width_piece = piece.shape[1]
    anchor = position * col_count

    def visit(b, running):
        portion = lax.dynamic_slice_in_dim(piece, b * col_count, col_count, 1)
        return absorb(running, left_feat, portion, anchor - b * col_count)

    final = lax.fori_loop(0, width_piece // col_count, visit, start_state)
    return finish(final, col_count)


def solution(mesh):
    in_specs = (P("row", "col", None), P("row", "col", None), P())
    out_specs = (P("row", "col"), P("row", "col"))
    return jax.shard_map(local, mesh=mesh, in_specs=in_specs, out_specs=out_specs, check_vma=False)
```

profile of v0, /device:TPU:1, one launch (start us, length us, event | category | flops | bytes accessed | tf_op | source)
XLA Modules:
  0.0 227.8 jit_solution(3837790933711198921)
XLA Ops:
  8.8 4.9 %collective-permute-start = (bf16[2,8,1,128]{3,1,2,0:T(8,128)(2,1)S(1)}, bf16[2,8,1,128]{3,1,2,0:T(8,128)(2,1)S(1)}, u32[]{:S(2)}, u32[]{:S(2)}) collective-permute-start(bf16[2,8,1,128]{3,1,2,0:T(8,128)(2,1)S(1)} %pad_maximum_fusion.3), channel_id=1, source_target_pairs={{0,1},{1,2},{2,3},{3,4},{4,5},{5,6},{6,7},{7,8},{8,9},{9,10},{10,1... | collective-permute-start | bytes 12296 | tf_op jit(solution)/shard_map/ppermute | solution.py:12
  15.6 3.8 %collective-permute-start.1 = (bf16[2,1,513,128]{3,2,1,0:T(8,128)(2,1)S(1)}, bf16[2,1,513,128]{3,2,1,0:T(8,128)(2,1)}, u32[]{:S(2)}, u32[]{:S(2)}) collective-permute-start(bf16[2,1,513,128]{3,2,1,0:T(8,128)(2,1)S(1)} %pad_maximum_fusion.2), channel_id=1, source_target_pairs={{0,32},{32,64},{64,96},{96,128},{128,160},{160,192},{192,224},{1,3... | collective-permute-start | bytes 787976 | tf_op jit(solution)/shard_map/ppermute | solution.py:12
  19.4 2.6 %slice.131 = bf16[4,256,128]{2,1,0:T(8,128)(2,1)} slice(bf16[8,512,128]{2,1,0:T(8,128)(2,1)S(1)} %copy-done), slice={[0:7:2], [1:512:2], [0:128:1]} | slice | bytes 524288 | tf_op jit(solution)/shard_map/slice | solution.py:19
  22.0 2.6 %slice.129 = bf16[4,256,128]{2,1,0:T(8,128)(2,1)} slice(bf16[8,512,128]{2,1,0:T(8,128)(2,1)S(1)} %copy-done), slice={[0:7:2], [0:511:2], [0:128:1]} | slice | bytes 524288 | tf_op jit(solution)/shard_map/slice | solution.py:19
  24.6 2.7 %slice.137 = bf16[4,256,128]{2,1,0:T(8,128)(2,1)} slice(bf16[8,512,128]{2,1,0:T(8,128)(2,1)S(1)} %copy-done), slice={[1:8:2], [1:512:2], [0:128:1]} | slice | bytes 524288 | tf_op jit(solution)/shard_map/slice | solution.py:19
  27.4 2.7 %slice.135 = bf16[4,256,128]{2,1,0:T(8,128)(2,1)} slice(bf16[8,512,128]{2,1,0:T(8,128)(2,1)S(1)} %copy-done), slice={[1:8:2], [0:511:2], [0:128:1]} | slice | bytes 524288 | tf_op jit(solution)/shard_map/slice | solution.py:19
  30.4 2.7 %slice.133 = bf16[4,256,128]{2,1,0:T(8,128)(2,1)} slice(bf16[8,513,128]{2,1,0:T(8,128)(2,1)S(1)} %pad_maximum_fusion.1), slice={[1:8:2], [0:511:2], [0:128:1]} | slice | bytes 524288 | tf_op jit(solution)/shard_map/slice | solution.py:19
  33.1 2.6 %slice.127 = bf16[4,256,128]{2,1,0:T(8,128)(2,1)} slice(bf16[8,513,128]{2,1,0:T(8,128)(2,1)S(1)} %pad_maximum_fusion.1), slice={[0:7:2], [0:511:2], [0:128:1]} | slice | bytes 524288 | tf_op jit(solution)/shard_map/slice | solution.py:19
  37.0 2.6 %slice.125 = bf16[4,256,128]{2,1,0:T(8,128)(2,1)} slice(bf16[9,513,128]{2,1,0:T(8,128)(2,1)S(1)} %maximum_maximum_fusion), slice={[0:7:2], [2:513:2], [0:128:1]} | slice | bytes 524288 | tf_op jit(solution)/shard_map/slice | solution.py:19
  40.0 2.6 %slice.121 = bf16[4,256,128]{2,1,0:T(8,128)(2,1)} slice(bf16[9,513,128]{2,1,0:T(8,128)(2,1)S(1)} %maximum_maximum_fusion), slice={[0:7:2], [0:511:2], [0:128:1]} | slice | bytes 524288 | tf_op jit(solution)/shard_map/slice | solution.py:19
  51.7 2.6 %slice.145 = bf16[4,256,128]{2,1,0:T(8,128)(2,1)} slice(bf16[8,512,128]{2,1,0:T(8,128)(2,1)S(1)} %copy-done.1), slice={[0:7:2], [1:512:2], [0:128:1]} | slice | bytes 524288 | tf_op jit(solution)/shard_map/slice | solution.py:19
  54.3 2.6 %slice.144 = bf16[4,256,128]{2,1,0:T(8,128)(2,1)} slice(bf16[8,512,128]{2,1,0:T(8,128)(2,1)S(1)} %copy-done.1), slice={[0:7:2], [0:511:2], [0:128:1]} | slice | bytes 524288 | tf_op jit(solution)/shard_map/slice | solution.py:19
  58.3 2.7 %slice.146 = bf16[4,256,128]{2,1,0:T(8,128)(2,1)} slice(bf16[8,513,128]{2,1,0:T(8,128)(2,1)S(1)} %pad_maximum_fusion), slice={[1:8:2], [0:511:2], [0:128:1]} | slice | bytes 524288 | tf_op jit(solution)/shard_map/slice | solution.py:19
  61.0 2.6 %slice.143 = bf16[4,256,128]{2,1,0:T(8,128)(2,1)} slice(bf16[8,513,128]{2,1,0:T(8,128)(2,1)S(1)} %pad_maximum_fusion), slice={[0:7:2], [0:511:2], [0:128:1]} | slice | bytes 524288 | tf_op jit(solution)/shard_map/slice | solution.py:19
  70.4 85.2 %all-gather.2.cloned.1.call-done = bf16[4,8192,256]{2,1,0:T(8,128)(2,1)} async-done(((bf16[4,256,256]{2,1,0:T(8,128)(2,1)}), bf16[4,8192,256]{2,1,0:T(8,128)(2,1)}) %all-gather.2.cloned.1.call-update) | async-done | bytes 16777232 | tf_op jit(solution)/shard_map/all_gather | solution.py:77
  155.5 64.8 %while.20 = (s32[]{:T(128)}, f32[4,256]{1,0:T(4,128)S(1)}, f32[4,256]{1,0:T(4,128)S(1)}, f32[4,256]{1,0:T(4,128)S(1)}, f32[4,256]{1,0:T(4,128)S(1)}, /*index=5*/...) while((s32[]{:T(128)}, f32[4,256]{1,0:T(4,128)S(1)}, ...), condition=%wide.region_5.6_spmd.clone, body=%wide.region_0.5_spmd.clone.sunk | while | flops 137309440 | bytes 3955922 | solution.py:85
  157.7 1.4 select_reduce_fusion.2
  163.8 1.4 select_reduce_fusion.2
  167.8 1.4 select_reduce_fusion.2
  171.9 1.4 select_reduce_fusion.2
  175.9 1.4 select_reduce_fusion.2
  180.0 1.4 select_reduce_fusion.2
  188.1 1.4 select_reduce_fusion.2
  192.1 1.4 select_reduce_fusion.2
  (324 shorter events, 74.4 us)
Async XLA Ops:
  7.2 8.3 %copy-start.1 = (bf16[8,512,128]{2,1,0:T(8,128)(2,1)S(1)}, bf16[8,512,128]{2,1,0:T(8,128)(2,1)}, u32[]{:S(2)}) copy-start(bf16[8,512,128]{2,1,0:T(8,128)(2,1)} %param.5) | copy-start | bytes 3145732
  7.2 148.4 %all-gather.2.cloned.1.call-start = ((), (), s32[]{:S(2)}) async-start(), calls=%async_computation | async-start | bytes 17301504 | tf_op jit(solution)/shard_map/all_gather | solution.py:77
  8.8 5.7 %collective-permute-start = (bf16[2,8,1,128]{3,1,2,0:T(8,128)(2,1)S(1)}, bf16[2,8,1,128]{3,1,2,0:T(8,128)(2,1)S(1)}, u32[]{:S(2)}, u32[]{:S(2)}) collective-permute-start(bf16[2,8,1,128]{3,1,2,0:T(8,128)(2,1)S(1)} %pad_maximum_fusion.3), channel_id=1, source_target_pairs={{0,1},{1,2},{2,3},{3,4},{4,5},{5,6},{6,7},{7,8},{8,9},{9,10},{10,1... | collective-permute-start | bytes 12296 | tf_op jit(solution)/shard_map/ppermute | solution.py:12
  14.5 5.0 %copy-start = (bf16[8,512,128]{2,1,0:T(8,128)(2,1)S(1)}, bf16[8,512,128]{2,1,0:T(8,128)(2,1)}, u32[]{:S(2)}) copy-start(bf16[8,512,128]{2,1,0:T(8,128)(2,1)} %param.6) | copy-start | bytes 3145732
  15.6 20.1 %collective-permute-start.1 = (bf16[2,1,513,128]{3,2,1,0:T(8,128)(2,1)S(1)}, bf16[2,1,513,128]{3,2,1,0:T(8,128)(2,1)}, u32[]{:S(2)}, u32[]{:S(2)}) collective-permute-start(bf16[2,1,513,128]{3,2,1,0:T(8,128)(2,1)S(1)} %pad_maximum_fusion.2), channel_id=1, source_target_pairs={{0,32},{32,64},{64,96},{96,128},{128,160},{160,192},{192,224},{1,3... | collective-permute-start | bytes 787976 | tf_op jit(solution)/shard_map/ppermute | solution.py:12
  37.0 5.6 %copy-start.2 = (bf16[3,3,128,256]{3,2,1,0:T(8,128)(2,1)S(1)}, bf16[3,3,128,256]{3,2,1,0:T(8,128)(2,1)}, u32[]{:S(2)}) copy-start(bf16[3,3,128,256]{3,2,1,0:T(8,128)(2,1)} %param.7) | copy-start | bytes 1769476
  43.9 1.0 copy-start.12
  44.8 0.9 copy-start.10
  45.8 0.9 copy-start.8
  46.7 0.9 copy-start.5
  47.7 0.9 copy-start.6
  48.6 0.9 copy-start.3
  49.6 0.9 copy-start.13
  65.7 1.0 copy-start.11
  66.6 1.0 copy-start.7
  67.6 0.9 copy-start.4
  68.6 0.9 copy-start.9
Sparse Core Ops, SparseCore 0:
  51.8 103.7 all-gather.1
where the time goes:
time: 230 us; the launch traced here: 228 us
  waiting for transfers between devices  85.9 us (37%)
  matrix products  51.6 us (22%)
  local copies, waits for them, and re-layouts  44.5 us (19%)
  other arithmetic  20.5 us (9%)
  between operations  14.3 us (6%)
  starting transfers between devices  8.8 us (4%)
    all_gather x1, waiting for transfers between devices, local(): piece = lax.all_gather(right_feat, 'col', axis=1, tiled=True)  85.2 us
    dot_general x32, matrix products, absorb(): jnp.einsum('rif,rjf->rij', query, panel_keys, preferred_element_type=jnp....  44.9 us
    slice x18, local copies, waits for them, and re-layouts, conv_taps(): window = padded[a:a + 2 * row_count - 1:2, b:b + 2 * col_count - 1:2, :]  34.4 us
    reduce_sum x32, other arithmetic, absorb(): jnp.sum(weights * settled, axis=-1)  12.7 us
    ppermute x2, starting transfers between devices, from_behind(): return lax.ppermute(array, axis, pairs)  8.76 us
    unnamed x28, local copies, waits for them, and re-layouts  7.4 us
    dot_general x18, matrix products, conv_taps(): jnp.dot(window.reshape(row_count * col_count, -1), weights[a, b], preferr...  6.72 us
  transfers between devices with their start and end apart: 3, of which 2 were waited for; matrix products, arithmetic and copies ran while one was open for 14% of the time, Pallas kernels for 0%

commit v1 on v0

--- a/solution.py
+++ b/solution.py
@@ -74,7 +74,9 @@
     right_feat = conv_taps(right_full, conv_weight, row_count, col_count)
     position = lax.axis_index("col")
     start_state = empty_state(row_count, col_count)
-    piece = lax.all_gather(right_feat, "col", axis=1, tiled=True)
+    piece = jnp.concatenate(
+        lax.all_to_all(jnp.stack([right_feat] * lax.axis_size("col")), "col", 0, 0), axis=1
+    )
     width_piece = piece.shape[1]
     anchor = position * col_count
 

time: 230 us -> 502 us (2.18)
  the two profiles are of different devices: /device:TPU:1 before, /device:TPU:102 now
where the time goes in v1:
time: 502 us; the launch traced here: 500 us
  waiting for transfers between devices  358 us (71%)
  local copies, waits for them, and re-layouts  52.2 us (10%)
  matrix products  49.9 us (10%)
  other arithmetic  20.4 us (4%)
  starting transfers between devices  16.3 us (3%)
    all_to_all x1, waiting for transfers between devices, local(): lax.all_to_all(jnp.stack([right_feat] * lax.axis_size('col')), 'col', 0, 0)  355 us
    dot_general x32, matrix products, absorb(): jnp.einsum('rif,rjf->rij', query, panel_keys, preferred_element_type=jnp....  44.9 us
    slice x18, local copies, waits for them, and re-layouts, conv_taps(): window = padded[a:a + 2 * row_count - 1:2, b:b + 2 * col_count - 1:2, :]  25.4 us
    all_to_all x1, local copies, waits for them, and re-layouts, local(): lax.all_to_all(jnp.stack([right_feat] * lax.axis_size('col')), 'col', 0, 0)  13.9 us
    reduce_sum x32, other arithmetic, absorb(): jnp.sum(weights * settled, axis=-1)  12.6 us
  transfers between devices with their start and end apart: 3, of which 2 were waited for; matrix products, arithmetic and copies ran while one was open for 6% of the time, Pallas kernels for 0%

profile of v1, /device:TPU:102, one launch (start us, length us, event | category | flops | bytes accessed | tf_op | source)
XLA Modules:
  0.0 499.7 jit_solution(16991476140624722128)
XLA Ops:
  2.2 1.9 collective-permute-start
  4.1 3.0 collective-permute-done
  8.2 5.0 %collective-permute-start.1 = (bf16[2,1,513,128]{3,2,1,0:T(8,128)(2,1)S(1)}, bf16[2,1,513,128]{3,2,1,0:T(8,128)(2,1)S(1)}, u32[]{:S(2)}, u32[]{:S(2)}) collective-permute-start(bf16[2,1,513,128]{3,2,1,0:T(8,128)(2,1)S(1)} %pad_maximum_fusion.2), channel_id=1, source_target_pairs={{0,32},{32,64},{64,96},{96,128},{128,160},{160,192},{192,224},{1,3... | collective-permute-start | bytes 787976 | tf_op jit(solution)/shard_map/ppermute | solution.py:12
  13.2 2.6 slice.129
  16.8 2.7 slice.137
  19.8 2.6 slice.127
  22.4 2.7 slice.133
  31.8 5.9 %stack.27 = bf16[32,4,256,256]{3,2,1,0:T(8,128)(2,1)} broadcast(bf16[4,256,256]{2,1,0:T(8,128)(2,1)S(1)} %bitcast.108), dimensions={1,2,3} | broadcast | bytes 17301504 | tf_op jit(solution)/shard_map/stack | solution.py:78
  37.8 9.3 %all-to-all-start = ((bf16[32,4,256,256]{3,2,1,0:T(8,128)(2,1)}), bf16[32,4,256,256]{3,2,1,0:T(8,128)(2,1)}, u32[]{:S(2)}, u32[]{:S(2)}) async-start(bf16[32,4,256,256]{3,2,1,0:T(8,128)(2,1)} %stack.27), calls=%async_computation | async-start | bytes 33554432 | tf_op jit(solution)/shard_map/all_to_all | solution.py:78
  47.1 2.6 slice.144
  50.7 2.7 slice.148
  53.7 2.6 slice.143
  56.3 2.7 slice.146
  65.7 354.6 %all-to-all-done = bf16[32,4,256,256]{3,2,1,0:T(8,128)(2,1)} async-done(((bf16[32,4,256,256]{3,2,1,0:T(8,128)(2,1)}), bf16[32,4,256,256]{3,2,1,0:T(8,128)(2,1)}, u32[]{:S(2)}, u32[]{:S(2)}) %all-to-all-start) | async-done | bytes 16777248 | tf_op jit(solution)/shard_map/all_to_all | solution.py:78
  420.3 13.9 %copy.20 = bf16[32,4,256,256]{3,2,0,1:T(8,128)(2,1)} copy(bf16[32,4,256,256]{3,2,1,0:T(8,128)(2,1)} %all-to-all-done) | data formatting | bytes 33554432 | tf_op jit(solution)/shard_map/all_to_all | solution.py:78
  434.2 64.9 %while.20 = (s32[]{:T(128)}, f32[4,256]{1,0:T(4,128)S(1)}, f32[4,256]{1,0:T(4,128)S(1)}, f32[4,256]{1,0:T(4,128)S(1)}, f32[4,256]{1,0:T(4,128)S(1)}, /*index=5*/...) while((s32[]{:T(128)}, f32[4,256]{1,0:T(4,128)S(1)}, ...), condition=%wide.region_5.6_spmd.clone, body=%wide.region_0.5_spmd.clone.sunk | while | flops 137309440 | bytes 3955914 | solution.py:87
  442.4 1.4 select_reduce_fusion.2
  446.4 1.4 select_reduce_fusion.2
  456.6 1.4 select_reduce_fusion.2
  460.6 1.4 select_reduce_fusion.2
  470.8 1.4 select_reduce_fusion.2
  474.8 1.4 select_reduce_fusion.2
  485.0 1.4 select_reduce_fusion.2
  489.0 1.4 select_reduce_fusion.2
  (319 shorter events, 70.2 us)
Async XLA Ops:
  0.6 7.5 %copy-start = (bf16[8,512,128]{2,1,0:T(8,128)(2,1)S(1)}, bf16[8,512,128]{2,1,0:T(8,128)(2,1)}, u32[]{:S(2)}) copy-start(bf16[8,512,128]{2,1,0:T(8,128)(2,1)} %param.6) | copy-start | bytes 3145732
  2.2 4.9 collective-permute-start
  8.2 16.9 %collective-permute-start.1 = (bf16[2,1,513,128]{3,2,1,0:T(8,128)(2,1)S(1)}, bf16[2,1,513,128]{3,2,1,0:T(8,128)(2,1)S(1)}, u32[]{:S(2)}, u32[]{:S(2)}) collective-permute-start(bf16[2,1,513,128]{3,2,1,0:T(8,128)(2,1)S(1)} %pad_maximum_fusion.2), channel_id=1, source_target_pairs={{0,32},{32,64},{64,96},{96,128},{128,160},{160,192},{192,224},{1,3... | collective-permute-start | bytes 787976 | tf_op jit(solution)/shard_map/ppermute | solution.py:12
  25.4 1.2 copy-start.2
  27.2 1.0 copy-start.7
  28.1 0.9 copy-start.4
  29.3 1.0 copy-start.5
  30.6 1.0 copy-start.10
  37.8 9.4 %copy-start.1 = (bf16[8,512,128]{2,1,0:T(8,128)(2,1)S(1)}, bf16[8,512,128]{2,1,0:T(8,128)(2,1)}, u32[]{:S(2)}) copy-start(bf16[8,512,128]{2,1,0:T(8,128)(2,1)} %param.5) | copy-start | bytes 3145732
  37.8 382.5 %all-to-all-start = ((bf16[32,4,256,256]{3,2,1,0:T(8,128)(2,1)}), bf16[32,4,256,256]{3,2,1,0:T(8,128)(2,1)}, u32[]{:S(2)}, u32[]{:S(2)}) async-start(bf16[32,4,256,256]{3,2,1,0:T(8,128)(2,1)} %stack.27), calls=%async_computation | async-start | bytes 33554432 | tf_op jit(solution)/shard_map/all_to_all | solution.py:78
  61.0 1.0 copy-start.8
  62.0 0.9 copy-start.3
  63.2 1.0 copy-start.6
  64.4 1.0 copy-start.9
